TPU v7x, 32 devices: a whole 2x2x4 slice. The times are simulated.
32 devices in a mesh: groups: 2 (over y), ctx: 4 (over z), head: 2 (over x), rep: 2 (over core).
Axes of the slice: x: 2, y: 2, z: 4, core: 2. Of those that a mesh axis runs over, the one named last changes fastest.
Arguments:
- queries: bfloat16 [4, 512, 1024], P(('groups', 'rep'), 'ctx', 'head'), parts along dimension 0, may hold values from -6 to 6
- per_head_keys: bfloat16 [4, 512, 1024], P(('groups', 'rep'), 'ctx', 'head'), parts along dimension 0, may hold values from -6 to 6
- value_rows: bfloat16 [4, 512, 1024], P(('groups', 'rep'), 'ctx', 'head'), parts along dimension 0, may hold values from -6 to 6
- gate_logits: bfloat16 [4, 512, 1024], P(('groups', 'rep'), 'ctx', 'head'), parts along dimension 0, may hold values from -16 to 4
- gate_bias: float32 [1024], P('head'), may hold values from -1 to 13
- value_weight: float32 [1024], P('head'), may hold values from -0.1875 to 0.1875
- targets: float32 [4, 512], P(('groups', 'rep'), 'ctx'), parts along dimension 0, may hold values from -6 to 6
- mask_ids: int32 [4, 4], P(('groups', 'rep'), 'ctx'), parts along dimension 0, may hold values from 0 to 3
- segment_starts: int32 [4, 512], P(('groups', 'rep'), 'ctx'), parts along dimension 0, may hold values 0 or 1
Outputs:
- value_pred: float32 [4, 512], P(('groups', 'rep'), 'ctx'), parts along dimension 0
- query_gradient_rows: bfloat16 [4, 512, 1024], P(('groups', 'rep'), 'ctx', 'head'), parts along dimension 0
- grad_keys: bfloat16 [4, 512, 1024], P(('groups', 'rep'), 'ctx', 'head'), parts along dimension 0
- grad_values: bfloat16 [4, 512, 1024], P(('groups', 'rep'), 'ctx', 'head'), parts along dimension 0
- grad_gate_logits: bfloat16 [4, 512, 1024], P(('groups', 'rep'), 'ctx', 'head'), parts along dimension 0
- grad_gate_bias: float32 [2048], P(('groups', 'head')), parts along dimension 0
- grad_value_weight: float32 [2048], P(('groups', 'head')), parts along dimension 0
There are 2 independent parts, one for each index of `groups`. A program takes and returns all parts, laid end to end along the dimension named above; an argument that names none is the same for every part. Nothing has to cross between parts.
Inputs may be any that keep to these rules, and one draw needn't show every extreme that they name: `mask_ids`: the window kind of each block of 128 positions. `segment_starts`: flags of segment starts.
All inputs are finite; a program needn't handle non-finite values. No bound on the sum of `segment_starts` on one device may be relied on, other than what follows from the above.
Results may differ from a plain program's by a relative error of at most 0.013.
Values sent between devices are 32-bit elements; how exact they have to be, the bound alone decides.
No kernel may reach another device: no remote copies, remote signals or barrier semaphores. Data moves between devices by JAX's collectives and lax.ppermute only.
A program may use at most 64 MiB of HBM per device.

v0:
```python
import jax
import jax.numpy as jnp
from jax import lax
from jax.sharding import PartitionSpec as P

DK = 128
DV = 128
epsilon = 1.0
gate_scale = 16.0
highest = lax.Precision.HIGHEST


def from_behind(value, axis, by):
    length = lax.axis_size(axis)
    pairs = [(i, i + by) for i in range(length) if 0 <= i + by < length]
    return lax.ppermute(value, axis, pairs)


def block_pass(query_in, key_in, value_in, decay, start_flags, kind_ids):
    blocks = kind_ids.shape[0]
    block_len = query_in.shape[0] // blocks
    head_count = query_in.shape[1]
    channels = query_in.shape[2]
    value_width = value_in.shape[2]
    query_f = query_in.astype(jnp.float32).reshape(blocks, block_len, head_count, channels)
    key_f = key_in.astype(jnp.float32).reshape(blocks, block_len, head_count, channels)
    value_bf = value_in.reshape(blocks, block_len, head_count, value_width)
    value_f = value_bf.astype(jnp.float32)
    log_cum = jnp.cumsum(decay.reshape(blocks, block_len, head_count, channels), axis=1)
    log_last = log_cum[:, -1]
    segment = jnp.cumsum(start_flags.reshape(blocks, block_len), axis=1, dtype=jnp.int32)
    alive_mask = (segment == 0).astype(jnp.float32)
    offsets = jnp.arange(block_len, dtype=jnp.int32)
    distance = offsets[:, None] - offsets[None, :]
    window = block_len // jnp.left_shift(jnp.ones_like(kind_ids), kind_ids)
    live_pairs = (
        (segment[:, :, None] == segment[:, None, :])
        & (distance[None] >= 0)
        & (distance[None] < window[:, None, None])
    )
    query_dec = query_f * jnp.exp(log_cum) * channels ** (-0.5)
    key_dec = key_f * jnp.exp(-log_cum)
    scores = jnp.einsum("bihc,bjhc->bhij", query_dec, key_dec, precision=highest)
    block_probs = jnp.where(live_pairs[:, None], scores, 0.0).astype(jnp.bfloat16)
    inner_part = jnp.einsum(
        "bhij,bjhd->bihd", block_probs, value_bf, preferred_element_type=jnp.float32
    )
    tail_mask = (segment == segment[:, -1:]).astype(jnp.float32)
    key_tail = key_f * jnp.exp(log_last[:, None] - log_cum) * tail_mask[:, :, None, None]
    block_state = jnp.einsum("bjhc,bjhd->bhcd", key_tail, value_f, precision=highest)
    block_decay = jnp.exp(log_last) * alive_mask[:, -1][:, None, None]

    def advance(carried_in, block_items):
        state_now, factor = carried_in
        new_state = state_now * block_items[1][..., None] + block_items[0]
        return ((new_state, factor * block_items[1]), (state_now, factor))

    initial = (
        jnp.zeros((head_count, channels, value_width), jnp.float32),
        jnp.ones((head_count, channels), jnp.float32),
    )
    finals, befores = lax.scan(advance, initial, (block_state, block_decay))
    query_live = query_dec * alive_mask[:, :, None, None]
    outer_part = jnp.einsum("bihc,bhcd->bihd", query_live, befores[0], precision=highest)
    carried = query_live * befores[1][:, None]
    attended = (inner_part + outer_part).reshape(blocks * block_len, head_count, value_width)
    return (
        attended,
        finals[0],
        finals[1],
        carried.reshape(blocks * block_len, head_count, channels),
    )


def on_device(
    queries,
    per_head_keys,
    value_rows,
    gate_logits,
    gate_bias,
    value_weight,
    targets,
    mask_ids,
    segment_starts,
):
    token_count = queries.shape[1]
    head_count = gate_bias.shape[0] // DK

    def to_heads(array):
        return array[0].reshape(token_count, head_count, -1)

    start_flags = segment_starts[0]
    kind_ids = mask_ids[0]

    def local_terms(query_in, key_in, value_in, logit_in, bias_in):
        decay = jax.nn.log_sigmoid(logit_in.astype(jnp.float32) + bias_in) / gate_scale
        return block_pass(query_in, key_in, value_in, decay, start_flags, kind_ids)

    local_out, pull_local = jax.vjp(
        local_terms,
        to_heads(queries),
        to_heads(per_head_keys),
        to_heads(value_rows),
        to_heads(gate_logits),
        gate_bias.reshape(head_count, DK),
    )
    attended_local, state_local, decay_local, carried = local_out

    def pass_state(position, incoming):
        return from_behind(incoming * decay_local[..., None] + state_local, "ctx", 1)

    state_in = lax.fori_loop(0, lax.axis_size("ctx") - 1, pass_state, jnp.zeros_like(state_local))
    attended = attended_local + jnp.einsum("thc,hcd->thd", carried, state_in, precision=highest)

    def value_head(attended_in, weight_in):
        normed = attended_in * lax.rsqrt(
            jnp.mean(attended_in * attended_in, axis=-1, keepdims=True) + epsilon
        )
        return jnp.einsum("thd,hd->t", normed, weight_in, precision=highest)

    partial_value, pull_value = jax.vjp(value_head, attended, value_weight.reshape(head_count, DV))
    value_pred = lax.psum(partial_value, "head")
    residual = value_pred - targets[0]
    grad_attended, grad_weight = pull_value(residual)
    grad_carried = jnp.einsum("thd,hcd->thc", grad_attended, state_in, precision=highest)
    grad_direct = jnp.einsum("thc,thd->hcd", carried, grad_attended, precision=highest)

    def pass_grad(position, incoming):
        return from_behind(grad_direct + decay_local[..., None] * incoming, "ctx", -1)

    grad_state = lax.fori_loop(0, lax.axis_size("ctx") - 1, pass_grad, jnp.zeros_like(grad_direct))
    grad_decay = jnp.sum(state_in * grad_state, axis=-1)
    grad_query, grad_key, grad_value, grad_logit, grad_bias = pull_local(
        (grad_attended, grad_state, grad_decay, grad_carried)
    )
    token_total = token_count * lax.axis_size("ctx") * lax.axis_size("rep")
    bias_total, weight_total = lax.psum(
        (grad_bias.reshape(-1), grad_weight.reshape(-1)), ("ctx", "rep")
    )
    return (
        value_pred[None],
        grad_query.reshape(1, token_count, -1),
        grad_key.reshape(1, token_count, -1),
        grad_value.reshape(1, token_count, -1),
        grad_logit.reshape(1, token_count, -1),
        bias_total / token_total,
        weight_total / token_total,
    )


def solution(mesh):
    in_specs = (
        P(("groups", "rep"), "ctx", "head"),
        P(("groups", "rep"), "ctx", "head"),
        P(("groups", "rep"), "ctx", "head"),
        P(("groups", "rep"), "ctx", "head"),
        P("head"),
        P("head"),
        P(("groups", "rep"), "ctx"),
        P(("groups", "rep"), "ctx"),
        P(("groups", "rep"), "ctx"),
    )
    out_specs = (
        P(("groups", "rep"), "ctx"),
        P(("groups", "rep"), "ctx", "head"),
        P(("groups", "rep"), "ctx", "head"),
        P(("groups", "rep"), "ctx", "head"),
        P(("groups", "rep"), "ctx", "head"),
        P(("groups", "head")),
        P(("groups", "head")),
    )
    return jax.shard_map(
        on_device, mesh=mesh, in_specs=in_specs, out_specs=out_specs, check_vma=False
    )
```

profile of v0, /device:TPU:0, one launch (start us, length us, event | category | flops | bytes accessed | tf_op | source)
XLA Modules:
  0.0 105.6 jit_solution(13447743507898511805)
XLA Ops:
  0.6 1.0 reshape.486
  1.7 0.4 fusion.9
  2.0 0.6 copy-done.13
  2.7 0.3 reduce_window_sum.35
  3.0 0.6 slice.11
  4.2 0.6 slice.12
  4.8 1.2 %compare_convert_fusion.1 = (f32[128]{0:T(128)}, f32[128]{0:T(128)S(1)}) fusion(s32[1,128]{1,0:T(1,128)S(1)} %reduce_window_sum.35, s32[]{:T(128)} %bitcast.14), kind=kLoop, calls=%fused_computation.129 | loop fusion | flops 512 | bytes 1540 | tf_op jit(solution)/shard_map/jvp()/convert_element_type | solution.py:32
  6.3 0.8 copy-done.2
  7.1 0.5 convolution_add_fusion
  7.6 28.2 %while.4 = (s32[]{:T(128)}, f32[4,128,128]{2,1,0:T(8,128)S(1)}, f32[4,128]{1,0:T(4,128)S(1)}, f32[4,128,128]{2,1,0:T(8,128)S(1)}, s32[]{:T(128)}) while((s32[]{:T(128)}, f32[4,128,128]{2,1,0:T(8,128)S(1)}, f32[4,128]{1,0:T(4,128)S(1)}, f32[4,128,128]{2,1,0:T(8,128)S(1)}, s32[]{:T(128)}) %tuple.61), condition=%wide.region_3.4_spmd, body=%wide.region_2.3_spmd.sunk | while | flops 131074 | bytes 1837157 | solution.py:112
  7.6 0.1 multiply_add_fusion.5
  7.8 4.9 %collective-permute-start = (f32[4,128,128]{2,1,0:T(8,128)S(1)}, f32[4,128,128]{2,1,0:T(8,128)S(1)}, u32[]{:S(2)}, u32[]{:S(2)}) collective-permute-start(f32[4,128,128]{2,1,0:T(8,128)S(1)} %multiply_add_fusion.5), channel_id=1, source_target_pairs={{0,4},{4,8},{8,12},{1,5},{5,9},{9,13},{2,6},{6,10},{10,14},{3,7},{... | collective-permute-start | bytes 786440 | tf_op jit(solution)/shard_map/while/body/eval_jaxpr/ppermute | solution.py:16
  12.7 5.5 %collective-permute-done = f32[4,128,128]{2,1,0:T(8,128)S(1)} collective-permute-done((f32[4,128,128]{2,1,0:T(8,128)S(1)}, f32[4,128,128]{2,1,0:T(8,128)S(1)}, u32[]{:S(2)}, u32[]{:S(2)}) %collective-permute-start) | collective-permute-done | bytes 262176 | tf_op jit(solution)/shard_map/while/body/eval_jaxpr/ppermute | solution.py:16
  18.4 4.4 %collective-permute-start = (f32[4,128,128]{2,1,0:T(8,128)S(1)}, f32[4,128,128]{2,1,0:T(8,128)S(1)}, u32[]{:S(2)}, u32[]{:S(2)}) collective-permute-start(f32[4,128,128]{2,1,0:T(8,128)S(1)} %multiply_add_fusion.5), channel_id=1, source_target_pairs={{0,4},{4,8},{8,12},{1,5},{5,9},{9,13},{2,6},{6,10},{10,14},{3,7},{... | collective-permute-start | bytes 786440 | tf_op jit(solution)/shard_map/while/body/eval_jaxpr/ppermute | solution.py:16
  22.8 4.7 %collective-permute-done = f32[4,128,128]{2,1,0:T(8,128)S(1)} collective-permute-done((f32[4,128,128]{2,1,0:T(8,128)S(1)}, f32[4,128,128]{2,1,0:T(8,128)S(1)}, u32[]{:S(2)}, u32[]{:S(2)}) %collective-permute-start) | collective-permute-done | bytes 262176 | tf_op jit(solution)/shard_map/while/body/eval_jaxpr/ppermute | solution.py:16
  27.6 4.4 %collective-permute-start = (f32[4,128,128]{2,1,0:T(8,128)S(1)}, f32[4,128,128]{2,1,0:T(8,128)S(1)}, u32[]{:S(2)}, u32[]{:S(2)}) collective-permute-start(f32[4,128,128]{2,1,0:T(8,128)S(1)} %multiply_add_fusion.5), channel_id=1, source_target_pairs={{0,4},{4,8},{8,12},{1,5},{5,9},{9,13},{2,6},{6,10},{10,14},{3,7},{... | collective-permute-start | bytes 786440 | tf_op jit(solution)/shard_map/while/body/eval_jaxpr/ppermute | solution.py:16
  32.0 3.9 %collective-permute-done = f32[4,128,128]{2,1,0:T(8,128)S(1)} collective-permute-done((f32[4,128,128]{2,1,0:T(8,128)S(1)}, f32[4,128,128]{2,1,0:T(8,128)S(1)}, u32[]{:S(2)}, u32[]{:S(2)}) %collective-permute-start) | collective-permute-done | bytes 262176 | tf_op jit(solution)/shard_map/while/body/eval_jaxpr/ppermute | solution.py:16
  37.0 0.7 fusion.2
  37.7 0.2 convolution_bitcast_fusion.1
  37.9 0.7 fusion.1
  38.6 0.7 multiply_reduce_fusion.2
  39.4 0.6 copy-done.4
  40.0 0.2 convolution_bitcast_fusion.2
  40.3 4.9 %psum.21 = f32[128]{0:T(128)S(1)} all-reduce(f32[128]{0:T(128)S(1)} %convolution_bitcast_fusion.2), channel_id=1, replica_groups=mesh['groups'=2,'ctx'=4,'head'=2,'rep'=2] {'head'}, use_global_device_ids=true, to_apply=%region_5.6 | all-reduce | flops 128 | bytes 1024 | tf_op jit(solution)/shard_map/psum | solution.py:122
  45.2 0.5 copy-done.15
  45.7 0.1 fusion.6
  45.9 0.7 fusion.60
  46.6 28.3 %while.5 = (s32[]{:T(128)}, f32[4,128,128]{2,1,0:T(8,128)S(1)}, f32[4,128]{1,0:T(4,128)S(1)}, f32[4,128,128]{2,1,0:T(8,128)S(1)}, s32[]{:T(128)}) while((s32[]{:T(128)}, f32[4,128,128]{2,1,0:T(8,128)S(1)}, f32[4,128]{1,0:T(4,128)S(1)}, f32[4,128,128]{2,1,0:T(8,128)S(1)}, s32[]{:T(128)}) %tuple.67), condition=%wide.region_8.9_spmd, body=%wide.region_7.8_spmd.sunk | while | flops 131074 | bytes 1837157 | solution.py:131
  46.6 0.1 multiply_add_fusion.6
  46.8 1.3 %collective-permute-start.1 = (f32[4,128,128]{2,1,0:T(8,128)S(1)}, f32[4,128,128]{2,1,0:T(8,128)S(1)}, u32[]{:S(2)}, u32[]{:S(2)}) collective-permute-start(f32[4,128,128]{2,1,0:T(8,128)S(1)} %multiply_add_fusion.6), channel_id=1, source_target_pairs={{4,0},{8,4},{12,8},{5,1},{9,5},{13,9},{6,2},{10,6},{14,10},{7,3},{... | collective-permute-start | bytes 786440 | tf_op jit(solution)/shard_map/while/body/eval_jaxpr/ppermute | solution.py:16
  48.1 7.9 %collective-permute-done.1 = f32[4,128,128]{2,1,0:T(8,128)S(1)} collective-permute-done((f32[4,128,128]{2,1,0:T(8,128)S(1)}, f32[4,128,128]{2,1,0:T(8,128)S(1)}, u32[]{:S(2)}, u32[]{:S(2)}) %collective-permute-start.1) | collective-permute-done | bytes 262176 | tf_op jit(solution)/shard_map/while/body/eval_jaxpr/ppermute | solution.py:16
  55.9 0.1 multiply_add_fusion.6
  56.1 1.3 %collective-permute-start.1 = (f32[4,128,128]{2,1,0:T(8,128)S(1)}, f32[4,128,128]{2,1,0:T(8,128)S(1)}, u32[]{:S(2)}, u32[]{:S(2)}) collective-permute-start(f32[4,128,128]{2,1,0:T(8,128)S(1)} %multiply_add_fusion.6), channel_id=1, source_target_pairs={{4,0},{8,4},{12,8},{5,1},{9,5},{13,9},{6,2},{10,6},{14,10},{7,3},{... | collective-permute-start | bytes 786440 | tf_op jit(solution)/shard_map/while/body/eval_jaxpr/ppermute | solution.py:16
  57.4 8.8 %collective-permute-done.1 = f32[4,128,128]{2,1,0:T(8,128)S(1)} collective-permute-done((f32[4,128,128]{2,1,0:T(8,128)S(1)}, f32[4,128,128]{2,1,0:T(8,128)S(1)}, u32[]{:S(2)}, u32[]{:S(2)}) %collective-permute-start.1) | collective-permute-done | bytes 262176 | tf_op jit(solution)/shard_map/while/body/eval_jaxpr/ppermute | solution.py:16
  66.3 1.3 %collective-permute-start.1 = (f32[4,128,128]{2,1,0:T(8,128)S(1)}, f32[4,128,128]{2,1,0:T(8,128)S(1)}, u32[]{:S(2)}, u32[]{:S(2)}) collective-permute-start(f32[4,128,128]{2,1,0:T(8,128)S(1)} %multiply_add_fusion.6), channel_id=1, source_target_pairs={{4,0},{8,4},{12,8},{5,1},{9,5},{13,9},{6,2},{10,6},{14,10},{7,3},{... | collective-permute-start | bytes 786440 | tf_op jit(solution)/shard_map/while/body/eval_jaxpr/ppermute | solution.py:16
  67.6 7.3 %collective-permute-done.1 = f32[4,128,128]{2,1,0:T(8,128)S(1)} collective-permute-done((f32[4,128,128]{2,1,0:T(8,128)S(1)}, f32[4,128,128]{2,1,0:T(8,128)S(1)}, u32[]{:S(2)}, u32[]{:S(2)}) %collective-permute-start.1) | collective-permute-done | bytes 262176 | tf_op jit(solution)/shard_map/while/body/eval_jaxpr/ppermute | solution.py:16
  74.9 0.8 multiply_reduce_fusion
  75.7 0.5 fusion.100
  76.2 0.1 copy.140
  76.3 0.5 fusion.33
  76.8 0.1 copy.141
  77.0 0.3 fusion.4
  77.3 0.6 fusion.79
  77.9 0.8 copy.145
  78.8 0.6 fusion.56
  79.4 0.1 copy.151
  79.5 0.4 fusion.75
  79.9 0.1 copy.149
  80.1 0.1 copy.167
  80.2 1.4 %fusion.98 = (f32[4,128]{1,0:T(4,128)S(1)}, bf16[1,128,4,128]{3,2,1,0:T(4,128)(2,1)S(1)}, bf16[1,128,4,128]{3,2,1,0:T(4,128)(2,1)S(1)}, f32[1,128,4,128]{3,2,1,0:T(4,128)S(1)}) fusion(f32[1,128,4,128]{3,2,1,0:T(4,128)S(1)} %fusion.9, f32[4,128]{1,0:T(4,128)S(1)} %slice_bitcast_fusion, f32[1,128,4,128]{3,2,1,0:T(4,128)S(1)} %copy.167, f32[128]{0:T(128)} %copy-done.9, ...), kind=kLoop, calls=%fused_computation.145 | loop fusion | flops 1048064 | bytes 2364416 | tf_op jit(solution)/shard_map/transpose(jvp())/reduce_sum | solution.py:49
  81.7 0.1 copy.168
  81.8 0.7 copy-done
  82.6 0.8 reshape.491
  83.4 2.9 %fusion.55 = (f32[4,128]{1,0:T(4,128)S(1)}, f32[1,128,4,128]{3,2,1,0:T(4,128)S(1)}) fusion(f32[128,4,128]{2,1,0:T(4,128)} %reshape.491, f32[4,128]{1,0:T(4,128)S(1)} %bitcast.191, f32[1,128,4,128]{3,2,1,0:T(4,128)S(1)} %copy.167, f32[4,128,128]{2,0,1:T(4,128)S(1)} %copy.151, f32[1,1,4,128]{3,2,1,0:T(4,128)S(1)} %bitcast_add_fusion.2, ...), kind=kOutput, calls=%fused_computation.89 | output fusion | flops 10354176 | bytes 2105856 | tf_op jit(solution)/shard_map/transpose(jvp(jit(cumsum)))/reduce_window_sum | solution.py:29
  86.3 0.6 copy-done.6
  87.0 0.3 fusion.87
  87.3 13.6 %all-reduce.1 = (f32[512]{0:T(512)S(1)}, f32[512]{0:T(512)S(1)}) all-reduce(f32[512]{0:T(512)S(1)} %negate_bitcast_fusion, f32[512]{0:T(512)S(1)} %bitcast.192), channel_id=1, replica_groups=mesh['groups'=2,'ctx'=4,'head'=2,'rep'=2] {'ctx','rep'}, use_global_device_ids=true, to_apply=%region_14.15 | all-reduce | flops 1024 | bytes 8192 | tf_op jit(solution)/shard_map/psum | solution.py:137
  100.9 0.6 broadcast_multiply_fusion.1
  101.6 0.9 fusion.15
  102.5 0.6 convolution_convert_fusion
  103.1 0.3 fusion.5
  103.4 0.8 copy.155
  104.1 0.7 convert_element_type.156
  104.9 0.7 convert_element_type.158
  (51 shorter events, 1.4 us)
Async XLA Ops:
  0.6 1.0 copy-start.7
  1.6 4.3 %copy-start.1 = (bf16[1,128,512]{2,1,0:T(8,128)(2,1)S(1)}, bf16[1,128,512]{2,1,0:T(8,128)(2,1)}, u32[]{:S(2)}) copy-start(bf16[1,128,512]{2,1,0:T(8,128)(2,1)} %param.14) | copy-start | bytes 393220
  2.0 0.7 copy-start.13
  6.0 1.1 %copy-start.9 = (f32[128]{0:T(128)}, f32[128]{0:T(128)S(1)}, u32[]{:S(2)}) copy-start(f32[128]{0:T(128)S(1)} %get-tuple-element.174) | copy-start | bytes 1540
  6.1 0.9 copy-start.2
  7.6 29.0 %copy-start.3 = (bf16[1,128,512]{2,1,0:T(8,128)(2,1)S(1)}, bf16[1,128,512]{2,1,0:T(8,128)(2,1)}, u32[]{:S(2)}) copy-start(bf16[1,128,512]{2,1,0:T(8,128)(2,1)} %param.13) | copy-start | bytes 393220
  7.8 10.5 %collective-permute-start = (f32[4,128,128]{2,1,0:T(8,128)S(1)}, f32[4,128,128]{2,1,0:T(8,128)S(1)}, u32[]{:S(2)}, u32[]{:S(2)}) collective-permute-start(f32[4,128,128]{2,1,0:T(8,128)S(1)} %multiply_add_fusion.5), channel_id=1, source_target_pairs={{0,4},{4,8},{8,12},{1,5},{5,9},{9,13},{2,6},{6,10},{10,14},{3,7},{... | collective-permute-start | bytes 786440 | tf_op jit(solution)/shard_map/while/body/eval_jaxpr/ppermute | solution.py:16
  18.4 9.1 %collective-permute-start = (f32[4,128,128]{2,1,0:T(8,128)S(1)}, f32[4,128,128]{2,1,0:T(8,128)S(1)}, u32[]{:S(2)}, u32[]{:S(2)}) collective-permute-start(f32[4,128,128]{2,1,0:T(8,128)S(1)} %multiply_add_fusion.5), channel_id=1, source_target_pairs={{0,4},{4,8},{8,12},{1,5},{5,9},{9,13},{2,6},{6,10},{10,14},{3,7},{... | collective-permute-start | bytes 786440 | tf_op jit(solution)/shard_map/while/body/eval_jaxpr/ppermute | solution.py:16
  27.6 8.3 %collective-permute-start = (f32[4,128,128]{2,1,0:T(8,128)S(1)}, f32[4,128,128]{2,1,0:T(8,128)S(1)}, u32[]{:S(2)}, u32[]{:S(2)}) collective-permute-start(f32[4,128,128]{2,1,0:T(8,128)S(1)} %multiply_add_fusion.5), channel_id=1, source_target_pairs={{0,4},{4,8},{8,12},{1,5},{5,9},{9,13},{2,6},{6,10},{10,14},{3,7},{... | collective-permute-start | bytes 786440 | tf_op jit(solution)/shard_map/while/body/eval_jaxpr/ppermute | solution.py:16
  39.3 0.7 copy-start.4
  40.2 5.0 %copy-start.14 = (f32[1,128]{1,0:T(1,128)S(1)}, f32[1,128]{1,0:T(1,128)}, u32[]{:S(2)}) copy-start(f32[1,128]{1,0:T(1,128)} %param.19) | copy-start | bytes 1540
  45.2 0.5 copy-start.15
  45.7 31.3 %copy-start.5 = (f32[128]{0:T(128)}, f32[128]{0:T(128)S(1)}, u32[]{:S(2)}) copy-start(f32[128]{0:T(128)S(1)} %bitcast_subtract_fusion.1) | copy-start | bytes 1540
  46.8 9.2 %collective-permute-start.1 = (f32[4,128,128]{2,1,0:T(8,128)S(1)}, f32[4,128,128]{2,1,0:T(8,128)S(1)}, u32[]{:S(2)}, u32[]{:S(2)}) collective-permute-start(f32[4,128,128]{2,1,0:T(8,128)S(1)} %multiply_add_fusion.6), channel_id=1, source_target_pairs={{4,0},{8,4},{12,8},{5,1},{9,5},{13,9},{6,2},{10,6},{14,10},{7,3},{... | collective-permute-start | bytes 786440 | tf_op jit(solution)/shard_map/while/body/eval_jaxpr/ppermute | solution.py:16
  56.1 10.1 %collective-permute-start.1 = (f32[4,128,128]{2,1,0:T(8,128)S(1)}, f32[4,128,128]{2,1,0:T(8,128)S(1)}, u32[]{:S(2)}, u32[]{:S(2)}) collective-permute-start(f32[4,128,128]{2,1,0:T(8,128)S(1)} %multiply_add_fusion.6), channel_id=1, source_target_pairs={{4,0},{8,4},{12,8},{5,1},{9,5},{13,9},{6,2},{10,6},{14,10},{7,3},{... | collective-permute-start | bytes 786440 | tf_op jit(solution)/shard_map/while/body/eval_jaxpr/ppermute | solution.py:16
  66.3 8.6 %collective-permute-start.1 = (f32[4,128,128]{2,1,0:T(8,128)S(1)}, f32[4,128,128]{2,1,0:T(8,128)S(1)}, u32[]{:S(2)}, u32[]{:S(2)}) collective-permute-start(f32[4,128,128]{2,1,0:T(8,128)S(1)} %multiply_add_fusion.6), channel_id=1, source_target_pairs={{4,0},{8,4},{12,8},{5,1},{9,5},{13,9},{6,2},{10,6},{14,10},{7,3},{... | collective-permute-start | bytes 786440 | tf_op jit(solution)/shard_map/while/body/eval_jaxpr/ppermute | solution.py:16
  80.2 1.4 %copy-start.11 = (f32[4,128]{1,0:T(4,128)S(1)}, f32[4,128]{1,0:T(4,128)}, u32[]{:S(2)}) copy-start(f32[4,128]{1,0:T(4,128)} %get-tuple-element.145) | copy-start | bytes 6148
  80.2 1.4 %copy-start.12 = (f32[4,128]{1,0:T(4,128)S(1)}, f32[4,128]{1,0:T(4,128)}, u32[]{:S(2)}) copy-start(f32[4,128]{1,0:T(4,128)} %get-tuple-element.146) | copy-start | bytes 6148
  81.7 0.9 copy-start
  82.6 0.8 copy-start.8
  82.6 0.8 copy-start.10
  86.3 0.7 copy-start.6
where the time goes:
time: 106 us
  waiting for transfers between devices  38 us (36%)
  blocking collectives  18.5 us (17%)
  starting transfers between devices  17.6 us (17%)
  local copies, waits for them, and re-layouts  11.5 us (11%)
  other arithmetic  9.63 us (9%)
  matrix products  7.78 us (7%)
  between operations  2.37 us (2%)
    ppermute x6, waiting for transfers between devices, from_behind(): return lax.ppermute(value, axis, pairs)  38 us
    ppermute x6, starting transfers between devices, from_behind(): return lax.ppermute(value, axis, pairs)  17.6 us
    psum x1, blocking collectives, on_device(): lax.psum((grad_bias.reshape(-1), grad_weight.reshape(-1)), ('ctx', 'rep'))  13.6 us
    unnamed x35, local copies, waits for them, and re-layouts  5.02 us
    psum x1, blocking collectives, on_device(): value_pred = lax.psum(partial_value, 'head')  4.94 us
    another operation x2, other arithmetic, block_pass(): jnp.cumsum(decay.reshape(blocks, block_len, head_count, channels), axis=1)  3.28 us
  transfers between devices with their start and end apart: 6, of which 6 were waited for; matrix products, arithmetic and copies ran while one was open for 0% of the time, Pallas kernels for 0%

commit v1 on v0

--- a/solution.py
+++ b/solution.py
@@ -119,7 +119,7 @@
         return jnp.einsum("thd,hd->t", normed, weight_in, precision=highest)
 
     partial_value, pull_value = jax.vjp(value_head, attended, value_weight.reshape(head_count, DV))
-    value_pred = lax.psum(partial_value, "head")
+    value_pred = jnp.sum(lax.all_gather(partial_value, "head"), axis=0)
     residual = value_pred - targets[0]
     grad_attended, grad_weight = pull_value(residual)
     grad_carried = jnp.einsum("thd,hcd->thc", grad_attended, state_in, precision=highest)

time: 106 us -> 106 us (level)
    psum x1 -> x0, blocking collectives: 4.94 us -> none  [on_device(): value_pred = lax.psum(partial_value, 'head')]
    all_gather x0 -> x1, blocking collectives: none -> 4.22 us  [on_device(): value_pred = jnp.sum(lax.all_gather(partial_value, 'head'), axis=0)]
    unnamed x35 -> x39, local copies, waits for them, and re-layouts: 5.02 us -> 5.68 us
where the time goes in v1:
time: 106 us
  waiting for transfers between devices  38 us (36%)
  blocking collectives  17.8 us (17%)
  starting transfers between devices  17.6 us (17%)
  local copies, waits for them, and re-layouts  12.2 us (12%)
  other arithmetic  9.65 us (9%)
  matrix products  7.77 us (7%)
  between operations  2.37 us (2%)
    ppermute x6, waiting for transfers between devices, from_behind(): return lax.ppermute(value, axis, pairs)  38 us
    ppermute x6, starting transfers between devices, from_behind(): return lax.ppermute(value, axis, pairs)  17.6 us
    psum x1, blocking collectives, on_device(): lax.psum((grad_bias.reshape(-1), grad_weight.reshape(-1)), ('ctx', 'rep'))  13.6 us
    unnamed x39, local copies, waits for them, and re-layouts  5.68 us
    all_gather x1, blocking collectives, on_device(): value_pred = jnp.sum(lax.all_gather(partial_value, 'head'), axis=0)  4.22 us
    another operation x2, other arithmetic, block_pass(): jnp.cumsum(decay.reshape(blocks, block_len, head_count, channels), axis=1)  3.28 us
  transfers between devices with their start and end apart: 6, of which 6 were waited for; matrix products, arithmetic and copies ran while one was open for 0% of the time, Pallas kernels for 0%

profile of v1, /device:TPU:0, one launch (start us, length us, event | category | flops | bytes accessed | tf_op | source)
XLA Modules:
  0.0 105.5 jit_solution(18294157755191564867)
XLA Ops:
  0.6 1.0 reshape.488
  1.7 0.4 fusion.9
  2.0 0.6 copy-done.17
  2.7 0.3 reduce_window_sum.35
  3.0 0.6 slice.11
  4.2 0.6 slice.12
  4.8 1.2 %compare_convert_fusion.1 = (f32[128]{0:T(128)}, f32[128]{0:T(128)S(1)}) fusion(s32[1,128]{1,0:T(1,128)S(1)} %reduce_window_sum.35, s32[]{:T(128)} %bitcast.14), kind=kLoop, calls=%fused_computation.129 | loop fusion | flops 512 | bytes 1540 | tf_op jit(solution)/shard_map/jvp()/convert_element_type | solution.py:32
  6.3 0.8 copy-done.2
  7.1 0.5 convolution_add_fusion
  7.6 28.2 %while.4 = (s32[]{:T(128)}, f32[4,128,128]{2,1,0:T(8,128)S(1)}, f32[4,128]{1,0:T(4,128)S(1)}, f32[4,128,128]{2,1,0:T(8,128)S(1)}, s32[]{:T(128)}) while((s32[]{:T(128)}, f32[4,128,128]{2,1,0:T(8,128)S(1)}, f32[4,128]{1,0:T(4,128)S(1)}, f32[4,128,128]{2,1,0:T(8,128)S(1)}, s32[]{:T(128)}) %tuple.62), condition=%wide.region_3.4_spmd, body=%wide.region_2.3_spmd.sunk | while | flops 131074 | bytes 1837157 | solution.py:112
  7.6 0.1 multiply_add_fusion.5
  7.8 4.9 %collective-permute-start = (f32[4,128,128]{2,1,0:T(8,128)S(1)}, f32[4,128,128]{2,1,0:T(8,128)S(1)}, u32[]{:S(2)}, u32[]{:S(2)}) collective-permute-start(f32[4,128,128]{2,1,0:T(8,128)S(1)} %multiply_add_fusion.5), channel_id=1, source_target_pairs={{0,4},{4,8},{8,12},{1,5},{5,9},{9,13},{2,6},{6,10},{10,14},{3,7},{... | collective-permute-start | bytes 786440 | tf_op jit(solution)/shard_map/while/body/eval_jaxpr/ppermute | solution.py:16
  12.7 5.5 %collective-permute-done = f32[4,128,128]{2,1,0:T(8,128)S(1)} collective-permute-done((f32[4,128,128]{2,1,0:T(8,128)S(1)}, f32[4,128,128]{2,1,0:T(8,128)S(1)}, u32[]{:S(2)}, u32[]{:S(2)}) %collective-permute-start) | collective-permute-done | bytes 262176 | tf_op jit(solution)/shard_map/while/body/eval_jaxpr/ppermute | solution.py:16
  18.4 4.4 %collective-permute-start = (f32[4,128,128]{2,1,0:T(8,128)S(1)}, f32[4,128,128]{2,1,0:T(8,128)S(1)}, u32[]{:S(2)}, u32[]{:S(2)}) collective-permute-start(f32[4,128,128]{2,1,0:T(8,128)S(1)} %multiply_add_fusion.5), channel_id=1, source_target_pairs={{0,4},{4,8},{8,12},{1,5},{5,9},{9,13},{2,6},{6,10},{10,14},{3,7},{... | collective-permute-start | bytes 786440 | tf_op jit(solution)/shard_map/while/body/eval_jaxpr/ppermute | solution.py:16
  22.8 4.7 %collective-permute-done = f32[4,128,128]{2,1,0:T(8,128)S(1)} collective-permute-done((f32[4,128,128]{2,1,0:T(8,128)S(1)}, f32[4,128,128]{2,1,0:T(8,128)S(1)}, u32[]{:S(2)}, u32[]{:S(2)}) %collective-permute-start) | collective-permute-done | bytes 262176 | tf_op jit(solution)/shard_map/while/body/eval_jaxpr/ppermute | solution.py:16
  27.6 4.4 %collective-permute-start = (f32[4,128,128]{2,1,0:T(8,128)S(1)}, f32[4,128,128]{2,1,0:T(8,128)S(1)}, u32[]{:S(2)}, u32[]{:S(2)}) collective-permute-start(f32[4,128,128]{2,1,0:T(8,128)S(1)} %multiply_add_fusion.5), channel_id=1, source_target_pairs={{0,4},{4,8},{8,12},{1,5},{5,9},{9,13},{2,6},{6,10},{10,14},{3,7},{... | collective-permute-start | bytes 786440 | tf_op jit(solution)/shard_map/while/body/eval_jaxpr/ppermute | solution.py:16
  32.0 3.9 %collective-permute-done = f32[4,128,128]{2,1,0:T(8,128)S(1)} collective-permute-done((f32[4,128,128]{2,1,0:T(8,128)S(1)}, f32[4,128,128]{2,1,0:T(8,128)S(1)}, u32[]{:S(2)}, u32[]{:S(2)}) %collective-permute-start) | collective-permute-done | bytes 262176 | tf_op jit(solution)/shard_map/while/body/eval_jaxpr/ppermute | solution.py:16
  37.0 0.7 fusion.2
  37.7 0.2 convolution_bitcast_fusion.1
  37.9 0.7 fusion.1
  38.6 0.7 multiply_reduce_fusion.2
  39.4 0.6 copy-done.4
  40.0 0.2 convolution_bitcast_fusion.2
  40.2 4.2 %all-gather.1 = f32[2,1,128]{2,1,0:T(1,128)S(1)} all-gather(f32[1,1,128]{2,1,0:T(1,128)S(1)} %convolution_bitcast_fusion.2), channel_id=2, replica_groups=mesh['groups'=2,'ctx'=4,'head'=2,'rep'=2] {'head'}, dimensions={0}, use_global_device_ids=true | all-gather | bytes 1536 | tf_op jit(solution)/shard_map/all_gather | solution.py:122
  44.5 0.6 copy-done.15
  45.1 0.5 copy-done.13
  45.6 0.1 fusion.6
  45.8 0.7 fusion.60
  46.5 28.3 %while.5 = (s32[]{:T(128)}, f32[4,128,128]{2,1,0:T(8,128)S(1)}, f32[4,128]{1,0:T(4,128)S(1)}, f32[4,128,128]{2,1,0:T(8,128)S(1)}, s32[]{:T(128)}) while((s32[]{:T(128)}, f32[4,128,128]{2,1,0:T(8,128)S(1)}, f32[4,128]{1,0:T(4,128)S(1)}, f32[4,128,128]{2,1,0:T(8,128)S(1)}, s32[]{:T(128)}) %tuple.68), condition=%wide.region_8.9_spmd, body=%wide.region_7.8_spmd.sunk | while | flops 131074 | bytes 1837157 | solution.py:131
  46.5 0.1 multiply_add_fusion.6
  46.7 1.3 %collective-permute-start.1 = (f32[4,128,128]{2,1,0:T(8,128)S(1)}, f32[4,128,128]{2,1,0:T(8,128)S(1)}, u32[]{:S(2)}, u32[]{:S(2)}) collective-permute-start(f32[4,128,128]{2,1,0:T(8,128)S(1)} %multiply_add_fusion.6), channel_id=1, source_target_pairs={{4,0},{8,4},{12,8},{5,1},{9,5},{13,9},{6,2},{10,6},{14,10},{7,3},{... | collective-permute-start | bytes 786440 | tf_op jit(solution)/shard_map/while/body/eval_jaxpr/ppermute | solution.py:16
  48.0 7.9 %collective-permute-done.1 = f32[4,128,128]{2,1,0:T(8,128)S(1)} collective-permute-done((f32[4,128,128]{2,1,0:T(8,128)S(1)}, f32[4,128,128]{2,1,0:T(8,128)S(1)}, u32[]{:S(2)}, u32[]{:S(2)}) %collective-permute-start.1) | collective-permute-done | bytes 262176 | tf_op jit(solution)/shard_map/while/body/eval_jaxpr/ppermute | solution.py:16
  56.0 1.3 %collective-permute-start.1 = (f32[4,128,128]{2,1,0:T(8,128)S(1)}, f32[4,128,128]{2,1,0:T(8,128)S(1)}, u32[]{:S(2)}, u32[]{:S(2)}) collective-permute-start(f32[4,128,128]{2,1,0:T(8,128)S(1)} %multiply_add_fusion.6), channel_id=1, source_target_pairs={{4,0},{8,4},{12,8},{5,1},{9,5},{13,9},{6,2},{10,6},{14,10},{7,3},{... | collective-permute-start | bytes 786440 | tf_op jit(solution)/shard_map/while/body/eval_jaxpr/ppermute | solution.py:16
  57.3 8.8 %collective-permute-done.1 = f32[4,128,128]{2,1,0:T(8,128)S(1)} collective-permute-done((f32[4,128,128]{2,1,0:T(8,128)S(1)}, f32[4,128,128]{2,1,0:T(8,128)S(1)}, u32[]{:S(2)}, u32[]{:S(2)}) %collective-permute-start.1) | collective-permute-done | bytes 262176 | tf_op jit(solution)/shard_map/while/body/eval_jaxpr/ppermute | solution.py:16
  66.2 1.3 %collective-permute-start.1 = (f32[4,128,128]{2,1,0:T(8,128)S(1)}, f32[4,128,128]{2,1,0:T(8,128)S(1)}, u32[]{:S(2)}, u32[]{:S(2)}) collective-permute-start(f32[4,128,128]{2,1,0:T(8,128)S(1)} %multiply_add_fusion.6), channel_id=1, source_target_pairs={{4,0},{8,4},{12,8},{5,1},{9,5},{13,9},{6,2},{10,6},{14,10},{7,3},{... | collective-permute-start | bytes 786440 | tf_op jit(solution)/shard_map/while/body/eval_jaxpr/ppermute | solution.py:16
  67.5 7.3 %collective-permute-done.1 = f32[4,128,128]{2,1,0:T(8,128)S(1)} collective-permute-done((f32[4,128,128]{2,1,0:T(8,128)S(1)}, f32[4,128,128]{2,1,0:T(8,128)S(1)}, u32[]{:S(2)}, u32[]{:S(2)}) %collective-permute-start.1) | collective-permute-done | bytes 262176 | tf_op jit(solution)/shard_map/while/body/eval_jaxpr/ppermute | solution.py:16
  74.8 0.8 multiply_reduce_fusion
  75.6 0.5 fusion.101
  76.1 0.1 copy.171
  76.2 0.5 fusion.33
  76.7 0.1 copy.172
  76.9 0.3 fusion.4
  77.2 0.6 fusion.79
  77.8 0.8 copy.176
  78.7 0.6 fusion.56
  79.3 0.1 copy.182
  79.4 0.4 fusion.75
  79.8 0.1 copy.180
  80.0 0.1 copy.198
  80.2 1.4 %fusion.99 = (f32[4,128]{1,0:T(4,128)S(1)}, bf16[1,128,4,128]{3,2,1,0:T(4,128)(2,1)S(1)}, bf16[1,128,4,128]{3,2,1,0:T(4,128)(2,1)S(1)}, f32[1,128,4,128]{3,2,1,0:T(4,128)S(1)}) fusion(f32[1,128,4,128]{3,2,1,0:T(4,128)S(1)} %fusion.9, f32[4,128]{1,0:T(4,128)S(1)} %slice_bitcast_fusion, f32[1,128,4,128]{3,2,1,0:T(4,128)S(1)} %copy.198, f32[128]{0:T(128)} %copy-done.9, ...), kind=kLoop, calls=%fused_computation.146 | loop fusion | flops 1048064 | bytes 2364416 | tf_op jit(solution)/shard_map/transpose(jvp())/reduce_sum | solution.py:49
  81.6 0.1 copy.199
  81.8 0.7 copy-done
  82.5 0.8 reshape.493
  83.3 2.9 %fusion.55 = (f32[4,128]{1,0:T(4,128)S(1)}, f32[1,128,4,128]{3,2,1,0:T(4,128)S(1)}) fusion(f32[128,4,128]{2,1,0:T(4,128)} %reshape.493, f32[4,128]{1,0:T(4,128)S(1)} %bitcast.196, f32[1,128,4,128]{3,2,1,0:T(4,128)S(1)} %copy.198, f32[4,128,128]{2,0,1:T(4,128)S(1)} %copy.182, f32[1,1,4,128]{3,2,1,0:T(4,128)S(1)} %bitcast_add_fusion.2, ...), kind=kOutput, calls=%fused_computation.89 | output fusion | flops 10354176 | bytes 2105856 | tf_op jit(solution)/shard_map/transpose(jvp(jit(cumsum)))/reduce_window_sum | solution.py:29
  86.2 0.6 copy-done.14
  86.9 0.3 fusion.87
  87.2 13.6 %all-reduce.1 = (f32[512]{0:T(512)S(1)}, f32[512]{0:T(512)S(1)}) all-reduce(f32[512]{0:T(512)S(1)} %negate_bitcast_fusion, f32[512]{0:T(512)S(1)} %bitcast.197), channel_id=1, replica_groups=mesh['groups'=2,'ctx'=4,'head'=2,'rep'=2] {'ctx','rep'}, use_global_device_ids=true, to_apply=%region_14.15 | all-reduce | flops 1024 | bytes 8192 | tf_op jit(solution)/shard_map/psum | solution.py:137
  100.8 0.6 broadcast_multiply_fusion.1
  101.5 0.9 fusion.15
  102.4 0.6 convolution_convert_fusion
  103.1 0.3 fusion.5
  103.3 0.8 copy.186
  104.1 0.7 convert_element_type.156
  104.8 0.7 convert_element_type.158
  (56 shorter events, 1.6 us)
Async XLA Ops:
  0.6 1.0 copy-start.5
  1.6 4.3 %copy-start.1 = (bf16[1,128,512]{2,1,0:T(8,128)(2,1)S(1)}, bf16[1,128,512]{2,1,0:T(8,128)(2,1)}, u32[]{:S(2)}) copy-start(bf16[1,128,512]{2,1,0:T(8,128)(2,1)} %param.14) | copy-start | bytes 393220
  2.0 0.7 copy-start.17
  6.0 1.1 %copy-start.9 = (f32[128]{0:T(128)}, f32[128]{0:T(128)S(1)}, u32[]{:S(2)}) copy-start(f32[128]{0:T(128)S(1)} %get-tuple-element.181) | copy-start | bytes 1540
  6.1 0.9 copy-start.2
  7.6 29.0 %copy-start.3 = (bf16[1,128,512]{2,1,0:T(8,128)(2,1)S(1)}, bf16[1,128,512]{2,1,0:T(8,128)(2,1)}, u32[]{:S(2)}) copy-start(bf16[1,128,512]{2,1,0:T(8,128)(2,1)} %param.13) | copy-start | bytes 393220
  7.8 10.5 %collective-permute-start = (f32[4,128,128]{2,1,0:T(8,128)S(1)}, f32[4,128,128]{2,1,0:T(8,128)S(1)}, u32[]{:S(2)}, u32[]{:S(2)}) collective-permute-start(f32[4,128,128]{2,1,0:T(8,128)S(1)} %multiply_add_fusion.5), channel_id=1, source_target_pairs={{0,4},{4,8},{8,12},{1,5},{5,9},{9,13},{2,6},{6,10},{10,14},{3,7},{... | collective-permute-start | bytes 786440 | tf_op jit(solution)/shard_map/while/body/eval_jaxpr/ppermute | solution.py:16
  18.4 9.1 %collective-permute-start = (f32[4,128,128]{2,1,0:T(8,128)S(1)}, f32[4,128,128]{2,1,0:T(8,128)S(1)}, u32[]{:S(2)}, u32[]{:S(2)}) collective-permute-start(f32[4,128,128]{2,1,0:T(8,128)S(1)} %multiply_add_fusion.5), channel_id=1, source_target_pairs={{0,4},{4,8},{8,12},{1,5},{5,9},{9,13},{2,6},{6,10},{10,14},{3,7},{... | collective-permute-start | bytes 786440 | tf_op jit(solution)/shard_map/while/body/eval_jaxpr/ppermute | solution.py:16
  27.6 8.3 %collective-permute-start = (f32[4,128,128]{2,1,0:T(8,128)S(1)}, f32[4,128,128]{2,1,0:T(8,128)S(1)}, u32[]{:S(2)}, u32[]{:S(2)}) collective-permute-start(f32[4,128,128]{2,1,0:T(8,128)S(1)} %multiply_add_fusion.5), channel_id=1, source_target_pairs={{0,4},{4,8},{8,12},{1,5},{5,9},{9,13},{2,6},{6,10},{10,14},{3,7},{... | collective-permute-start | bytes 786440 | tf_op jit(solution)/shard_map/while/body/eval_jaxpr/ppermute | solution.py:16
  39.3 0.7 copy-start.4
  44.5 0.7 copy-start.15
  45.1 0.5 copy-start.13
  45.6 31.3 %copy-start.7 = (f32[128]{0:T(128)}, f32[128]{0:T(128)S(1)}, u32[]{:S(2)}) copy-start(f32[128]{0:T(128)S(1)} %subtract_bitcast_fusion) | copy-start | bytes 1540
  46.7 9.2 %collective-permute-start.1 = (f32[4,128,128]{2,1,0:T(8,128)S(1)}, f32[4,128,128]{2,1,0:T(8,128)S(1)}, u32[]{:S(2)}, u32[]{:S(2)}) collective-permute-start(f32[4,128,128]{2,1,0:T(8,128)S(1)} %multiply_add_fusion.6), channel_id=1, source_target_pairs={{4,0},{8,4},{12,8},{5,1},{9,5},{13,9},{6,2},{10,6},{14,10},{7,3},{... | collective-permute-start | bytes 786440 | tf_op jit(solution)/shard_map/while/body/eval_jaxpr/ppermute | solution.py:16
  56.0 10.1 %collective-permute-start.1 = (f32[4,128,128]{2,1,0:T(8,128)S(1)}, f32[4,128,128]{2,1,0:T(8,128)S(1)}, u32[]{:S(2)}, u32[]{:S(2)}) collective-permute-start(f32[4,128,128]{2,1,0:T(8,128)S(1)} %multiply_add_fusion.6), channel_id=1, source_target_pairs={{4,0},{8,4},{12,8},{5,1},{9,5},{13,9},{6,2},{10,6},{14,10},{7,3},{... | collective-permute-start | bytes 786440 | tf_op jit(solution)/shard_map/while/body/eval_jaxpr/ppermute | solution.py:16
  66.2 8.6 %collective-permute-start.1 = (f32[4,128,128]{2,1,0:T(8,128)S(1)}, f32[4,128,128]{2,1,0:T(8,128)S(1)}, u32[]{:S(2)}, u32[]{:S(2)}) collective-permute-start(f32[4,128,128]{2,1,0:T(8,128)S(1)} %multiply_add_fusion.6), channel_id=1, source_target_pairs={{4,0},{8,4},{12,8},{5,1},{9,5},{13,9},{6,2},{10,6},{14,10},{7,3},{... | collective-permute-start | bytes 786440 | tf_op jit(solution)/shard_map/while/body/eval_jaxpr/ppermute | solution.py:16
  80.1 1.4 %copy-start.11 = (f32[4,128]{1,0:T(4,128)S(1)}, f32[4,128]{1,0:T(4,128)}, u32[]{:S(2)}) copy-start(f32[4,128]{1,0:T(4,128)} %get-tuple-element.152) | copy-start | bytes 6148
  80.1 1.4 %copy-start.12 = (f32[4,128]{1,0:T(4,128)S(1)}, f32[4,128]{1,0:T(4,128)}, u32[]{:S(2)}) copy-start(f32[4,128]{1,0:T(4,128)} %get-tuple-element.153) | copy-start | bytes 6148
  81.6 0.9 copy-start
  82.5 0.8 copy-start.6
  82.5 0.8 copy-start.10
  86.2 0.7 copy-start.14
  86.2 0.7 copy-start.16
  102.4 0.7 copy-start.8
